TPU v7x, 32 devices: a whole 2x2x4 slice. The times are simulated.
32 devices in a mesh: dp: 8 (over y, x, core), tensor: 4 (over z).
Axes of the slice: x: 2, y: 2, z: 4, core: 2. Of those that a mesh axis runs over, the one named last changes fastest.
Arguments:
- tokens: bfloat16 [16384, 768], P(('dp', 'tensor')), may hold values from -6 to 6
- out_grad: bfloat16 [16384, 768], P(('dp', 'tensor')), may hold values from -6 to 6
- lengths: int32 [32], P('dp'), may hold values from 20 to 512, as said below
- qkv_weight: bfloat16 [3, 768, 768], P(None, None, 'tensor'), may hold values from -0.21875 to 0.21875
- qkv_bias: bfloat16 [2, 768], P(None, 'tensor'), may hold values from -3 to 3
- out_weight: bfloat16 [768, 768], P('tensor'), may hold values from -1.75 to 1.75
- out_bias: float32 [768], replicated, may hold values from -3 to 3
- norm1_gain: float32 [768], replicated, may hold values from 0.5 to 1.5
- norm1_shift: float32 [768], replicated, may hold values from -3 to 3
- up_weight: bfloat16 [768, 3072], P(None, 'tensor'), may hold values from -0.21875 to 0.21875
- up_bias: bfloat16 [3072], P('tensor'), may hold values from -3 to 3
- down_weight: bfloat16 [3072, 768], P('tensor'), may hold values from -0.109375 to 0.109375
- down_bias: float32 [768], replicated, may hold values from -3 to 3
- norm2_gain: float32 [768], replicated, may hold values from 0.5 to 1.5
- norm2_shift: float32 [768], replicated, may hold values from -3 to 3
Outputs:
- layer_out: bfloat16 [16384, 768], P(('dp', 'tensor'))
- input_grad: bfloat16 [16384, 768], P(('dp', 'tensor'))
- grad_qkv_weight: float32 [3, 768, 768], P(None, None, 'tensor')
- grad_qkv_bias: float32 [2, 768], P(None, 'tensor')
- grad_out_weight: float32 [768, 768], P('tensor')
- grad_out_bias: float32 [768], replicated
- grad_norm1_gain: float32 [768], replicated
- grad_norm1_shift: float32 [768], replicated
- grad_up_weight: float32 [768, 3072], P(None, 'tensor')
- grad_up_bias: float32 [3072], P('tensor')
- grad_down_weight: float32 [3072, 768], P('tensor')
- grad_down_bias: float32 [768], replicated
- grad_norm2_gain: float32 [768], replicated
- grad_norm2_shift: float32 [768], replicated
Inputs may be any that keep to these rules, and one draw needn't show every extreme that they name: Keys at positions lengths[p] and beyond of passage p are padding; some passage has exactly 512 and some exactly 20.
All inputs are finite; a program needn't handle non-finite values.
Results may differ from a plain program's by a relative error of at most 0.02.
Values may be sent and summed in bfloat16 or wider, within the bound.
No kernel may reach another device: no remote copies, remote signals or barrier semaphores. Data moves between devices by JAX's collectives and lax.ppermute only.
A program may use at most 128 MiB of HBM per device.

v0:
```python
import jax
import jax.numpy as jnp
from jax import lax
from jax.sharding import PartitionSpec as P

HD = 64
LEN = 512
EPS = 1e-12
NEG = -1e30


def layer_norm(values, gain_vec, shift_vec):
    center = values - jnp.mean(values, axis=-1, keepdims=True)
    spread = jnp.mean(center * center, axis=-1, keepdims=True)
    return center * lax.rsqrt(spread + EPS) * gain_vec + shift_vec


def gelu_exact(values):
    return jax.nn.gelu(values, approximate=False)


def contract(left, right, left_dim, right_dim):
    return lax.dot_general(
        left, right, (((left_dim,), (right_dim,)), ((), ())), preferred_element_type=jnp.float32
    )


def attend_forward(queries, key_rows, value_rows, usable, factor):
    scores = (
        jnp.einsum("pqhe,pkhe->phqk", queries, key_rows, preferred_element_type=jnp.float32)
        * factor
    )
    scores = jnp.where(usable[:, None, None, :], scores, NEG)
    log_total = jax.nn.logsumexp(scores, axis=-1, keepdims=True)
    attn_probs = jnp.exp(scores - log_total)
    context = jnp.einsum(
        "phqk,pkhe->pqhe",
        attn_probs.astype(jnp.bfloat16),
        value_rows,
        preferred_element_type=jnp.float32,
    )
    return (context, attn_probs)


def attend_backward(queries, key_rows, value_rows, attn_probs, context_grad, factor):
    prob_grad = jnp.einsum(
        "pqhe,pkhe->phqk", context_grad, value_rows, preferred_element_type=jnp.float32
    )
    row_dot = jnp.sum(prob_grad * attn_probs, axis=-1, keepdims=True)
    score_grad = (attn_probs * (prob_grad - row_dot)).astype(jnp.bfloat16)
    query_grad = (
        jnp.einsum("phqk,pkhe->pqhe", score_grad, key_rows, preferred_element_type=jnp.float32)
        * factor
    )
    key_grad = (
        jnp.einsum("phqk,pqhe->pkhe", score_grad, queries, preferred_element_type=jnp.float32)
        * factor
    )
    value_grad = jnp.einsum(
        "phqk,pqhe->pkhe",
        attn_probs.astype(jnp.bfloat16),
        context_grad,
        preferred_element_type=jnp.float32,
    )
    return (query_grad, key_grad, value_grad)


def dp_pow2(values, dp_size):
    steps = dp_size.bit_length() - 1
    return dp_size == 1 << steps and values.shape[0] % dp_size == 0


def dp_halve(values, dp_size, sum_dtype=None):
    steps = dp_size.bit_length() - 1
    index = lax.axis_index("dp")
    link = values.dtype
    kept = values if sum_dtype is None else values.astype(sum_dtype)
    for step in range(steps):
        bit = index >> step & 1
        half = kept.shape[0] // 2
        keep = lax.dynamic_slice_in_dim(kept, bit * half, half)
        give = lax.dynamic_slice_in_dim(kept, (1 - bit) * half, half).astype(link)
        got = lax.ppermute(give, "dp", [(i, i ^ 1 << step) for i in range(dp_size)])
        kept = keep + got.astype(kept.dtype)
    return kept


def bit_reversed(count):
    steps = count.bit_length() - 1
    return [int(format(i, f"0{steps}b")[::-1], 2) if steps else 0 for i in range(count)]


def dp_double(kept, dp_size):
    steps = dp_size.bit_length() - 1
    index = lax.axis_index("dp")
    for step in reversed(range(steps)):
        bit = index >> step & 1
        got = lax.ppermute(kept, "dp", [(i, i ^ 1 << step) for i in range(dp_size)])
        kept = jnp.concatenate([jnp.where(bit == 0, kept, got), jnp.where(bit == 0, got, kept)])
    return kept


def make_per_device(dp_size):

    def per_device(
        tokens,
        out_grad,
        lengths,
        qkv_weight,
        qkv_bias,
        out_weight,
        out_bias,
        norm1_gain,
        norm1_shift,
        up_weight,
        up_bias,
        down_weight,
        down_bias,
        norm2_gain,
        norm2_shift,
    ):
        rows, width = tokens.shape
        shard = qkv_weight.shape[2]
        groups = width // shard
        passages = rows // LEN
        heads = width // HD
        factor = HD ** (-0.5)
        packed_w = jnp.concatenate(
            [qkv_weight.reshape(3 * width, shard), out_weight.T, qkv_bias], axis=0
        )
        w_rows = packed_w.shape[0]
        half_rows = -(-w_rows // 16) * 8
        packed_w = jnp.pad(packed_w, ((0, 2 * half_rows - w_rows), (0, 0)))
        dp_index = lax.axis_index("dp")
        parity = dp_index % 2
        mine = lax.dynamic_slice_in_dim(packed_w, parity * half_rows, half_rows)
        mine = lax.all_gather(mine, "tensor", axis=0, tiled=False)
        other = lax.ppermute(mine, "dp", [(i, i ^ 1) for i in range(dp_size)])
        first = jnp.where(parity == 0, mine, other)
        second = jnp.where(parity == 0, other, mine)
        weights_all = jnp.concatenate([first, second], axis=1)[:, :w_rows]
        qkv_blocks = weights_all[:, : 3 * width].reshape(groups, 3, width, shard)
        proj_blocks = weights_all[:, 3 * width : 4 * width]
        bias_full = weights_all[:, 4 * width :].transpose(1, 0, 2).reshape(2, width)
        tensor_index = lax.axis_index("tensor")
        own_lengths = lax.dynamic_slice_in_dim(lengths, tensor_index * passages, passages)
        usable = jnp.arange(LEN, dtype=jnp.int32)[None, :] < own_lengths[:, None]
        own_tokens = tokens.astype(jnp.float32)
        projected = jnp.einsum(
            "rd,gtdj->trgj", tokens, qkv_blocks, preferred_element_type=jnp.float32
        ).reshape(3, rows, width)
        four_dims = (passages, LEN, heads, HD)
        queries = (projected[0] + bias_full[0]).astype(jnp.bfloat16).reshape(four_dims)
        key_rows = projected[1].astype(jnp.bfloat16).reshape(four_dims)
        value_rows = (projected[2] + bias_full[1]).astype(jnp.bfloat16).reshape(four_dims)
        context, attn_probs = attend_forward(queries, key_rows, value_rows, usable, factor)
        context_low = context.reshape(rows, width).astype(jnp.bfloat16)
        attn_out = jnp.einsum(
            "rgj,gcj->rc",
            context_low.reshape(rows, groups, shard),
            proj_blocks,
            preferred_element_type=jnp.float32,
        )
        middle, norm1_back = jax.vjp(
            layer_norm, own_tokens + attn_out + out_bias, norm1_gain, norm1_shift
        )
        middle_low = middle.astype(jnp.bfloat16)
        ffn_rows = lax.all_gather(middle_low, "tensor", axis=0, tiled=True)
        pre_act = jnp.dot(ffn_rows, up_weight, preferred_element_type=jnp.float32) + up_bias
        activated, gelu_back = jax.vjp(gelu_exact, pre_act)
        hidden = activated.astype(jnp.bfloat16)
        ffn_out = lax.psum_scatter(
            jnp.dot(hidden, down_weight, preferred_element_type=jnp.float32).astype(jnp.bfloat16),
            "tensor",
            scatter_dimension=0,
            tiled=True,
        ).astype(jnp.float32)
        layer_out, norm2_back = jax.vjp(
            layer_norm, middle + ffn_out + down_bias, norm2_gain, norm2_shift
        )
        second_grad, grad_norm2_gain, grad_norm2_shift = norm2_back(out_grad.astype(jnp.float32))
        branch_grad = second_grad.astype(jnp.bfloat16)
        grad_down_bias = jnp.sum(branch_grad, axis=0, dtype=jnp.float32)
        branch_rows = lax.all_gather(branch_grad, "tensor", axis=0, tiled=True)
        hidden_grad = contract(branch_rows, down_weight, 1, 1)
        grad_down_weight = contract(hidden, branch_rows, 0, 0)
        pre_grad = gelu_back(hidden_grad)[0].astype(jnp.bfloat16)
        grad_up_bias = jnp.sum(pre_grad, axis=0, dtype=jnp.float32)
        grad_up_weight = contract(ffn_rows, pre_grad, 0, 0)
        ffn_grads = (grad_up_weight, grad_down_weight)
        halved = all((dp_pow2(g, dp_size) for g in ffn_grads))
        if halved:
            ffn_grads = tuple((dp_halve(g, dp_size) for g in ffn_grads))
        else:
            ffn_grads = lax.psum(ffn_grads, "dp")
        middle_part = lax.psum_scatter(
            contract(pre_grad, up_weight, 1, 1).astype(jnp.bfloat16),
            "tensor",
            scatter_dimension=0,
            tiled=True,
        ).astype(jnp.float32)
        norm1_in, ffn_grads = lax.optimization_barrier((second_grad + middle_part, ffn_grads))
        first_grad, grad_norm1_gain, grad_norm1_shift = norm1_back(norm1_in)
        attn_grad = first_grad.astype(jnp.bfloat16)
        grad_out_bias = jnp.sum(attn_grad, axis=0, dtype=jnp.float32)
        context_grad = (
            jnp.einsum("rc,gcj->rgj", attn_grad, proj_blocks, preferred_element_type=jnp.float32)
            .astype(jnp.bfloat16)
            .reshape(four_dims)
        )
        early = contract(attn_grad, context_low, 0, 0)
        early_halved = dp_pow2(early, dp_size)
        if early_halved:
            early = dp_halve(early.astype(jnp.bfloat16), dp_size, jnp.float32)
        else:
            early = lax.psum_scatter(early, "dp", scatter_dimension=0, tiled=True)
        query_grad, key_grad, value_grad = attend_backward(
            queries, key_rows, value_rows, attn_probs, context_grad, factor
        )
        proj_grad = (
            jnp.stack([query_grad, key_grad, value_grad])
            .reshape(3, rows, width)
            .astype(jnp.bfloat16)
        )
        grad_bias_full = jnp.sum(proj_grad[0::2], axis=1, dtype=jnp.float32)
        grad_qkv_full = jnp.einsum(
            "rd,tre->tde", tokens, proj_grad, preferred_element_type=jnp.float32
        )
        input_part = jnp.einsum(
            "trgj,gtdj->rd",
            proj_grad.reshape(3, rows, groups, shard),
            qkv_blocks,
            preferred_element_type=jnp.float32,
        )
        input_grad = (first_grad + input_part).astype(jnp.bfloat16)
        small = jnp.stack(
            [
                grad_out_bias,
                grad_norm1_gain,
                grad_norm1_shift,
                grad_down_bias,
                grad_norm2_gain,
                grad_norm2_shift,
            ]
        )
        n_small = small.shape[0]
        small_rep = jnp.tile(small.reshape(n_small, groups, shard), (1, 1, groups)).reshape(
            n_small * groups, width
        )
        up_parts = grad_up_bias.shape[0] // shard
        own_group = (jnp.arange(width) // shard == tensor_index)[None, :]
        up_rep = jnp.where(
            own_group, jnp.tile(grad_up_bias.reshape(up_parts, shard), (1, groups)), 0.0
        )
        tail = jnp.concatenate([grad_bias_full, small_rep, up_rep], axis=0)
        tail_rows = tail.shape[0]
        tail = jnp.pad(tail, ((0, -(-tail_rows // 8) * 8 - tail_rows), (0, 0)))
        late = lax.psum_scatter(
            grad_qkv_full.reshape(3 * width, width).astype(jnp.bfloat16),
            "dp",
            scatter_dimension=0,
            tiled=True,
        ).astype(jnp.float32)
        joined = jnp.concatenate([late, early, tail], axis=0)
        joined = lax.psum_scatter(
            joined.reshape(joined.shape[0], groups, shard).transpose(1, 0, 2),
            "tensor",
            scatter_dimension=0,
            tiled=True,
        )[0]
        if halved:
            ffn_grads = tuple(
                (dp_double(g.astype(jnp.bfloat16), dp_size).astype(jnp.float32) for g in ffn_grads)
            )
            joined, ffn_grads = lax.optimization_barrier((joined, ffn_grads))
        grad_up_weight, grad_down_weight = ffn_grads
        late_rows = late.shape[0]
        early_rows = early.shape[0]
        joined = lax.all_gather(joined, "dp", axis=0, tiled=False)
        early = joined[:, late_rows : late_rows + early_rows]
        if early_halved:
            order = bit_reversed(dp_size)
            place = [order.index(b) for b in range(dp_size)]
            early = jnp.concatenate([early[p] for p in place], axis=0)
        pieces = [
            joined[:, :late_rows].reshape(-1, shard),
            early.reshape(-1, shard),
            jnp.sum(joined[:, late_rows + early_rows :], axis=0),
        ]
        grad_qkv_weight = pieces[0].reshape(3, width, shard)
        grad_out_weight = pieces[1].T
        tail = pieces[2]
        grad_qkv_bias = tail[:2]
        small_sum = tail[2 : 2 + n_small * groups].reshape(n_small, width)
        grad_up_bias = tail[2 + n_small * groups : 2 + n_small * groups + up_parts].reshape(-1)
        (
            grad_out_bias,
            grad_norm1_gain,
            grad_norm1_shift,
            grad_down_bias,
            grad_norm2_gain,
            grad_norm2_shift,
        ) = [small_sum[i] for i in range(n_small)]
        return (
            layer_out.astype(jnp.bfloat16),
            input_grad,
            grad_qkv_weight,
            grad_qkv_bias,
            grad_out_weight,
            grad_out_bias,
            grad_norm1_gain,
            grad_norm1_shift,
            grad_up_weight,
            grad_up_bias,
            grad_down_weight,
            grad_down_bias,
            grad_norm2_gain,
            grad_norm2_shift,
        )

    return per_device


def solution(mesh):
    placed = (
        P(("dp", "tensor"), None),
        P(("dp", "tensor"), None),
        P("dp"),
        P(None, None, "tensor"),
        P(None, "tensor"),
        P("tensor", None),
        P(),
        P(),
        P(),
        P(None, "tensor"),
        P("tensor"),
        P("tensor", None),
        P(),
        P(),
        P(),
    )
    return jax.shard_map(
        make_per_device(mesh.shape["dp"]),
        mesh=mesh,
        in_specs=placed,
        out_specs=(
            P(("dp", "tensor"), None),
            P(("dp", "tensor"), None),
            P(None, None, "tensor"),
            P(None, "tensor"),
            P("tensor", None),
            P(),
            P(),
            P(),
            P(None, "tensor"),
            P("tensor"),
            P("tensor", None),
            P(),
            P(),
            P(),
        ),
        check_vma=False,
    )
```

profile of v0, /device:TPU:0, one launch (start us, length us, event | category | flops | bytes accessed | tf_op | source)
XLA Modules:
  0.0 587.0 jit_solution(9950485908794336362)
XLA Ops:
  9.4 1.8 fusion.41
  11.3 56.9 %all-gather.13.cloned.1.call-done = bf16[4,1544,192]{1,2,0:T(8,128)(2,1)} async-done(((bf16[1,1544,192]{1,2,0:T(8,128)(2,1)}), bf16[4,1544,192]{1,2,0:T(8,128)(2,1)}) %all-gather.13.cloned.1.call-update) | async-done | bytes 2371600 | tf_op jit(solution)/shard_map/all_gather | solution.py:137
  69.5 3.9 collective-permute-done
  73.4 3.0 broadcast_select_fusion.1
  78.2 2.0 fusion.19
  80.4 1.5 fusion.56
  83.1 5.0 fusion
  88.1 2.6 exponential_reduce_fusion
  90.7 1.9 copy-done.2
  92.7 10.1 %fusion.1 = bf16[12,512,512]{1,2,0:T(8,128)(2,1)} fusion(f32[12,512,512]{1,2,0:T(8,128)} %copy-done.2, f32[12,512]{1,0:T(8,128)S(1)} %log_add_fusion, pred[512]{0:T(512)(128)(4,1)S(1)} %iota_compare_fusion.1), kind=kLoop, calls=%fused_computation.7 | loop fusion | flops 12582912 | bytes 18899456 | tf_op jit(solution)/shard_map/convert_element_type | solution.py:38
  102.8 4.1 convolution_convert_fusion.5
  107.0 2.7 fusion.58
  113.8 61.0 %all-gather.9.cloned.1.call-done = bf16[2048,768]{1,0:T(8,128)(2,1)} async-done(((bf16[512,768]{1,0:T(8,128)(2,1)}), bf16[2048,768]{1,0:T(8,128)(2,1)}) %all-gather.9.cloned.1.call-update) | async-done | bytes 3145744 | tf_op jit(solution)/shard_map/all_gather | solution.py:168
  174.8 18.5 %multiply_convert_fusion.1 = (bf16[2048,768]{1,0:T(8,128)(2,1)S(1)}, f32[2048,768]{1,0:T(8,128)}, f32[2048,768]{1,0:T(8,128)}) fusion(f32[768]{0:T(1024)} %convert_element_type.191, bf16[2048,768]{1,0:T(8,128)(2,1)} %all-gather.9.cloned.1.call-done, bf16[768,768]{1,0:T(8,128)(2,1)S(1)} %copy-done), kind=kOutput, calls=%fused_computation.11 | convolution fusion | flops 2519728128 | bytes 20057088 | tf_op jit(solution)/shard_map/dot_general | solution.py:169
  193.3 1.6 copy-done.49
  194.9 3.9 convolution_convert_fusion.1
  198.9 59.1 %reduce-scatter.5.cloned.1.call-done = bf16[512,768]{1,0:T(8,128)(2,1)} async-done(((bf16[2048,768]{1,0:T(8,128)(2,1)}), bf16[512,768]{1,0:T(8,128)(2,1)}) %reduce-scatter.5.cloned.1.call-update) | async-done | bytes 786448 | tf_op jit(solution)/shard_map/reduce_scatter | solution.py:172
  258.0 1.8 fusion.54
  261.4 1.6 fusion.53
  264.3 1.7 convert_reduce_fusion.3
  265.9 11.2 %reduce-scatter.7.cloned.1.call-start = ((), (), s32[]{:S(2)}) async-start(), calls=%async_computation.7 | async-start | bytes 3932160 | tf_op jit(solution)/shard_map/reduce_scatter | solution.py:196
  277.1 52.3 %all-gather.11.cloned.1.call-done = bf16[2048,768]{1,0:T(8,128)(2,1)} async-done(((bf16[512,768]{1,0:T(8,128)(2,1)}), bf16[2048,768]{1,0:T(8,128)(2,1)}) %all-gather.11.cloned.1.call-update) | async-done | bytes 3145744 | tf_op jit(solution)/shard_map/all_gather | solution.py:184
  329.5 11.0 %convert_reduce_fusion = (f32[768]{0:T(1024)}, bf16[2048,768]{1,0:T(8,128)(2,1)S(1)}) fusion(f32[2048,768]{1,0:T(8,128)} %get-tuple-element.89, f32[2048,768]{1,0:T(8,128)} %get-tuple-element.126, f32[768]{0:T(1024)} %convert_element_type.191, bf16[2048,768]{1,0:T(8,128)(2,1)} %all-gather.11.cloned.1.call-done, bf16[768,768]{1,0:T(8,128)(2,1)} %param.26), kind=kOutput, calls=%fused_computation.9 | convolution fusion | flops 2442657024 | bytes 20060160 | tf_op jit(solution)/shard_map/dot_general | solution.py:23
  340.5 1.7 copy-done.50
  342.2 4.0 convolution_convert_fusion
  346.3 5.7 fusion.60
  352.1 2.7 fusion.59
  357.2 2.5 collective-permute-done.4
  359.6 1.8 dynamic-slice_add_fusion
  362.3 1.5 collective-permute-start.5
  367.6 11.1 %collective-permute-done.5 = f32[192,768]{1,0:T(8,128)} collective-permute-done((f32[192,768]{1,0:T(8,128)}, f32[192,768]{1,0:T(8,128)}, u32[]{:S(2)}, u32[]{:S(2)}) %collective-permute-start.5) | collective-permute-done | bytes 589856 | tf_op jit(solution)/shard_map/ppermute | solution.py:83
  380.7 1.5 collective-permute-start.6
  382.2 8.4 %collective-permute-done.2 = f32[192,768]{1,0:T(8,128)} collective-permute-done((f32[192,768]{1,0:T(8,128)}, f32[192,768]{1,0:T(8,128)}, u32[]{:S(2)}, u32[]{:S(2)}) %collective-permute-start.2) | collective-permute-done | bytes 589856 | tf_op jit(solution)/shard_map/ppermute | solution.py:83
  392.5 1.5 collective-permute-start.3
  393.9 2.9 slice.148
  396.8 1.7 dynamic-slice_add_fusion.4
  398.5 2.5 collective-permute-done.3
  401.0 1.7 dynamic-slice_add_fusion.5
  402.6 2.8 reduce-scatter.7.cloned.1.call-done
  405.4 2.0 convert_add_fusion
  410.8 2.9 convolution_convert_fusion.4
  415.4 10.3 %multiply_reduce_fusion = (f32[12,512]{1,0:T(8,128)S(1)}, f32[12,512,512]{1,2,0:T(8,128)}) fusion(f32[12,512,512]{1,2,0:T(8,128)S(1)} %bitcast.136, f32[12,512]{1,0:T(8,128)S(1)} %copy-done.25, pred[512]{0:T(512)(128)(4,1)S(1)} %copy-done.40, bf16[512,12,64]{0,2,1:T(8,128)(2,1)S(1)} %bitcast.148, f32[512,12,64]{0,2,1:T(8,128)S(1)} %bitcast.140, ...), kind=kOutput, calls=%fused_computation.1 | convolution fusion | flops 419162112 | bytes 27577856 | tf_op jit(solution)/shard_map/pqhe,pkhe->phqk/dot_general | solution.py:46
  425.7 7.2 %multiply_convert_fusion = bf16[12,512,512]{1,2,0:T(8,128)(2,1)S(1)} fusion(f32[12,512,512]{1,2,0:T(8,128)} %get-tuple-element.128, f32[12,512,512]{1,2,0:T(8,128)S(1)} %bitcast.136, f32[12,512]{1,0:T(8,128)S(1)} %get-tuple-element.127, f32[12,512]{1,0:T(8,128)S(1)} %copy-done.25, pred[512]{0:T(512)(128)(4,1)S(1)} %copy-done.40), kind=kLoop, calls=%fused_computation | loop fusion | flops 18874368 | bytes 31506944 | tf_op jit(solution)/shard_map/convert_element_type | solution.py:50
  432.9 2.1 multiply_convert_fusion.2
  438.1 4.9 convolution_convert_fusion.2
  444.3 1.5 collective-permute-start.10
  446.4 2.2 fusion.28
  449.1 2.0 collective-permute-done.7
  452.9 7.4 %collective-permute-done.8 = bf16[192,768]{1,0:T(8,128)(2,1)S(1)} collective-permute-done((bf16[192,768]{1,0:T(8,128)(2,1)S(1)}, bf16[192,768]{1,0:T(8,128)(2,1)S(1)}, u32[]{:S(2)}, u32[]{:S(2)}) %collective-permute-start.8) | collective-permute-done | bytes 294944 | tf_op jit(solution)/shard_map/ppermute | solution.py:83
  462.0 3.6 collective-permute-done.9
  465.7 25.5 %reduce-scatter.9.cloned.1.call-done = bf16[288,768]{1,0:T(8,128)(2,1)} async-done(((bf16[2304,768]{1,0:T(8,128)(2,1)}), bf16[288,768]{1,0:T(8,128)(2,1)}) %reduce-scatter.9.cloned.1.call-update) | async-done | bytes 442384 | tf_op jit(solution)/shard_map/reduce_scatter | solution.py:258
  492.4 1.6 copy.94
  495.1 1.5 collective-permute-start.14
  498.3 6.7 %collective-permute-done.14 = bf16[192,768]{1,0:T(8,128)(2,1)S(1)} collective-permute-done((bf16[192,768]{1,0:T(8,128)(2,1)S(1)}, bf16[192,768]{1,0:T(8,128)(2,1)S(1)}, u32[]{:S(2)}, u32[]{:S(2)}) %collective-permute-start.14) | collective-permute-done | bytes 294944 | tf_op jit(solution)/shard_map/ppermute | solution.py:98
  506.0 4.1 collective-permute-done.11
  511.2 1.6 maximum_convert_fusion.1
  513.5 1.6 maximum_convert_fusion
  515.0 14.5 %reduce-scatter.11.cloned.1.call-done = f32[1,416,192]{1,2,0:T(8,128)} async-done(((f32[4,416,192]{1,2,0:T(8,128)}), f32[1,416,192]{1,2,0:T(8,128)}) %reduce-scatter.11.cloned.1.call-update) | async-done | bytes 319504 | tf_op jit(solution)/shard_map/reduce_scatter | solution.py:265
  529.6 5.2 fusion.26
  534.8 27.7 %all-gather.15.cloned.1.call-done = f32[8,416,192]{1,2,0:T(8,128)} async-done(((f32[1,416,192]{1,2,0:T(8,128)}), f32[8,416,192]{1,2,0:T(8,128)}) %all-gather.15.cloned.1.call-update) | async-done | bytes 2555920 | tf_op jit(solution)/shard_map/all_gather | solution.py:279
  569.9 3.2 slice.149
  573.2 2.2 copy.95
  575.4 1.8 copy.103
  577.2 1.5 slice_bitcast_fusion.1
  (245 shorter events, 53.3 us)
Async XLA Ops:
  7.2 167.6 %copy-start = (bf16[768,768]{1,0:T(8,128)(2,1)S(1)}, bf16[768,768]{1,0:T(8,128)(2,1)}, u32[]{:S(2)}) copy-start(bf16[768,768]{1,0:T(8,128)(2,1)} %param.24) | copy-start | bytes 3538948
  7.2 61.1 %copy-start.48 = (s32[4]{0:T(128)S(1)}, s32[4]{0:T(128)}, u32[]{:S(2)}) copy-start(s32[4]{0:T(128)} %param.17) | copy-start | bytes 52
  7.2 61.1 %all-gather.13.cloned.1.call-start = ((), (), s32[]{:S(2)}) async-start(), calls=%async_computation.10 | async-start | bytes 3194880 | tf_op jit(solution)/shard_map/all_gather | solution.py:137
  11.3 163.5 %all-gather.9.cloned.1.call-start = ((), (), s32[]{:S(2)}) async-start(), calls=%async_computation.4 | async-start | bytes 3932160 | tf_op jit(solution)/shard_map/all_gather | solution.py:168
  68.3 5.2 collective-permute-start
  69.5 23.2 %copy-start.39 = (pred[512]{0:T(512)(128)(4,1)}, pred[512]{0:T(512)(128)(4,1)S(1)}, u32[]{:S(2)}) copy-start(pred[512]{0:T(512)(128)(4,1)S(1)} %iota_compare_fusion.1) | copy-start | bytes 1540
  77.9 2.4 copy-start.12
  81.9 20.9 %copy-start.4 = (f32[1,512,4,192]{1,3,0,2:T(8,128)}, f32[1,512,4,192]{1,3,0,2:T(8,128)S(1)}, u32[]{:S(2)}) copy-start(f32[1,512,4,192]{1,3,0,2:T(8,128)S(1)} %get-tuple-element.92) | copy-start | bytes 4718596
  88.1 4.6 copy-start.2
  92.7 10.1 %copy-start.24 = (f32[12,512]{1,0:T(8,128)}, f32[12,512]{1,0:T(8,128)S(1)}, u32[]{:S(2)}) copy-start(f32[12,512]{1,0:T(8,128)S(1)} %log_add_fusion) | copy-start | bytes 73732
  92.7 10.1 %copy-start.26 = (f32[12,64]{1,0:T(8,128)S(1)}, f32[12,64]{1,0:T(8,128)}, u32[]{:S(2)}) copy-start(f32[12,64]{1,0:T(8,128)} %reshape.335) | copy-start | bytes 9220
  102.8 4.1 copy-start.46
  102.8 4.1 copy-start.47
  106.9 2.8 copy-start.16
  107.0 4.3 copy-start.28
  107.0 4.2 copy-start.34
  112.4 145.6 %reduce-scatter.5.cloned.1.call-start = ((), (), s32[]{:S(2)}) async-start(), calls=%async_computation.5 | async-start | bytes 3932160 | tf_op jit(solution)/shard_map/reduce_scatter | solution.py:172
  174.8 20.1 %copy-start.44 = (bf16[768,768]{1,0:T(8,128)(2,1)S(1)}, bf16[768,768]{1,0:T(8,128)(2,1)}, u32[]{:S(2)}) copy-start(bf16[768,768]{1,0:T(8,128)(2,1)} %param.26) | copy-start | bytes 3538948
  198.9 130.6 %all-gather.11.cloned.1.call-start = ((), (), s32[]{:S(2)}) async-start(), calls=%async_computation.6 | async-start | bytes 3932160 | tf_op jit(solution)/shard_map/all_gather | solution.py:184
  258.0 2.2 copy-start.15
  258.0 2.2 copy-start.35
  263.1 2.9 copy-start.31
  265.9 139.5 %reduce-scatter.7.cloned.1.call-start = ((), (), s32[]{:S(2)}) async-start(), calls=%async_computation.7 | async-start | bytes 3932160 | tf_op jit(solution)/shard_map/reduce_scatter | solution.py:196
  346.3 144.9 %reduce-scatter.9.cloned.1.call-start = ((), (), s32[]{:S(2)}) async-start(), calls=%async_computation.8 | async-start | bytes 3981312 | tf_op jit(solution)/shard_map/reduce_scatter | solution.py:258
  346.3 5.7 copy-start.43
  346.3 5.7 copy-start.51
  352.1 2.8 copy-start.20
  354.8 1.8 copy-start.18
  356.6 3.0 collective-permute-start.4
  356.6 7.1 %collective-permute-start.1 = (f32[384,768]{1,0:T(8,128)}, f32[384,768]{1,0:T(8,128)}, u32[]{:S(2)}, u32[]{:S(2)}) collective-permute-start(f32[384,768]{1,0:T(8,128)} %get-tuple-element.130), channel_id=1, source_target_pairs={{0,4},{4,0},{8,12},{12,8},{16,20},{20,16},{24,28},{28,24},{1,5},{5... | collective-permute-start | bytes 3538952 | tf_op jit(solution)/shard_map/ppermute | solution.py:83
  357.2 6.6 %copy-start.19 = (f32[768,768]{1,0:T(8,128)S(1)}, f32[768,768]{1,0:T(8,128)}, u32[]{:S(2)}) copy-start(f32[768,768]{1,0:T(8,128)} %copy-done.18) | copy-start | bytes 7077892
  362.3 16.5 %collective-permute-start.5 = (f32[192,768]{1,0:T(8,128)}, f32[192,768]{1,0:T(8,128)}, u32[]{:S(2)}, u32[]{:S(2)}) collective-permute-start(f32[192,768]{1,0:T(8,128)} %constant_dynamic-slice_fusion.1), channel_id=1, source_target_pairs={{0,8},{4,12},{8,0},{12,4},{16,24},{20,28},{24,16},{28,20},{1,9},{5... | collective-permute-start | bytes 1769480 | tf_op jit(solution)/shard_map/ppermute | solution.py:83
  367.0 23.5 %collective-permute-start.2 = (f32[192,768]{1,0:T(8,128)}, f32[192,768]{1,0:T(8,128)}, u32[]{:S(2)}, u32[]{:S(2)}) collective-permute-start(f32[192,768]{1,0:T(8,128)} %constant_dynamic-slice_fusion.4), channel_id=1, source_target_pairs={{0,8},{4,12},{8,0},{12,4},{16,24},{20,28},{24,16},{28,20},{1,9},{5... | collective-permute-start | bytes 1769480 | tf_op jit(solution)/shard_map/ppermute | solution.py:83
  367.6 23.0 %copy-start.11 = (f32[384,768]{1,0:T(8,128)S(1)}, f32[384,768]{1,0:T(8,128)}, u32[]{:S(2)}) copy-start(f32[384,768]{1,0:T(8,128)} %copy-done.10) | copy-start | bytes 3538948
  379.9 11.8 %copy-start.21 = (f32[192,768]{1,0:T(8,128)}, f32[192,768]{1,0:T(8,128)S(1)}, u32[]{:S(2)}) copy-start(f32[192,768]{1,0:T(8,128)S(1)} %dynamic-slice_add_fusion.2) | copy-start | bytes 1769476
  380.7 16.1 %collective-permute-start.6 = (f32[96,768]{1,0:T(8,128)}, f32[96,768]{1,0:T(8,128)}, u32[]{:S(2)}, u32[]{:S(2)}) collective-permute-start(f32[96,768]{1,0:T(8,128)} %constant_dynamic-slice_fusion), channel_id=1, source_target_pairs={{0,16},{4,20},{8,24},{12,28},{16,0},{20,4},{24,8},{28,12},{1,17},{... | collective-permute-start | bytes 884744 | tf_op jit(solution)/shard_map/ppermute | solution.py:83
  392.5 4.3 copy-start.22
  392.5 8.5 %collective-permute-start.3 = (f32[96,768]{1,0:T(8,128)}, f32[96,768]{1,0:T(8,128)}, u32[]{:S(2)}, u32[]{:S(2)}) collective-permute-start(f32[96,768]{1,0:T(8,128)} %constant_dynamic-slice_fusion.3), channel_id=1, source_target_pairs={{0,16},{4,20},{8,24},{12,28},{16,0},{20,4},{24,8},{28,12},{1,17},{... | collective-permute-start | bytes 884744 | tf_op jit(solution)/shard_map/ppermute | solution.py:83
  398.5 9.0 %copy-start.30 = (f32[512]{0:T(512)S(1)}, f32[512]{0:T(512)}, u32[]{:S(2)}) copy-start(f32[512]{0:T(512)} %copy-done.29) | copy-start | bytes 6148
  405.4 4.9 slice-start.3
  408.2 2.6 slice-start.4
  408.2 5.6 slice-start
  409.4 4.3 slice-start.1
  410.8 4.2 slice-start.2
  410.8 4.6 copy-start.5
  410.8 4.6 copy-start.25
  410.8 4.6 copy-start.27
  410.8 4.6 copy-start.40
  425.7 7.2 %copy-start.7 = (f32[1,512,4,192]{1,3,0,2:T(8,128)S(1)}, f32[1,512,4,192]{1,3,0,2:T(8,128)}, u32[]{:S(2)}) copy-start(f32[1,512,4,192]{1,3,0,2:T(8,128)} %get-tuple-element.93) | copy-start | bytes 4718596
  435.0 2.6 copy-start.13
  443.1 86.5 %reduce-scatter.11.cloned.1.call-start = ((), (), s32[]{:S(2)}) async-start(), calls=%async_computation.9 | async-start | bytes 1966080 | tf_op jit(solution)/shard_map/reduce_scatter | solution.py:265
  444.3 52.3 %collective-permute-start.10 = (bf16[96,768]{1,0:T(8,128)(2,1)}, bf16[96,768]{1,0:T(8,128)(2,1)}, u32[]{:S(2)}, u32[]{:S(2)}) collective-permute-start(bf16[96,768]{1,0:T(8,128)(2,1)} %dynamic-slice_add_fusion.5), channel_id=1, source_target_pairs={{0,16},{4,20},{8,24},{12,28},{16,0},{20,4},{24,8},{28,12},{1,17},{... | collective-permute-start | bytes 442376 | tf_op jit(solution)/shard_map/ppermute | solution.py:98
  445.8 48.2 %collective-permute-start.13 = (bf16[96,768]{1,0:T(8,128)(2,1)}, bf16[96,768]{1,0:T(8,128)(2,1)}, u32[]{:S(2)}, u32[]{:S(2)}) collective-permute-start(bf16[96,768]{1,0:T(8,128)(2,1)} %dynamic-slice_add_fusion.4), channel_id=1, source_target_pairs={{0,16},{4,20},{8,24},{12,28},{16,0},{20,4},{24,8},{28,12},{1,17},{... | collective-permute-start | bytes 442376 | tf_op jit(solution)/shard_map/ppermute | solution.py:98
  448.7 2.4 collective-permute-start.7
  451.2 9.1 %collective-permute-start.8 = (bf16[192,768]{1,0:T(8,128)(2,1)S(1)}, bf16[192,768]{1,0:T(8,128)(2,1)S(1)}, u32[]{:S(2)}, u32[]{:S(2)}) collective-permute-start(bf16[192,768]{1,0:T(8,128)(2,1)S(1)} %dynamic-slice_convert_fusion.1), channel_id=1, source_target_pairs={{0,8},{4,12},{8,0},{12,4},{16,24},{20,28},{24,16},{28,20},{1,9},{5... | collective-permute-start | bytes 884744 | tf_op jit(solution)/shard_map/ppermute | solution.py:83
  460.4 5.2 collective-permute-start.9
  494.0 68.5 %all-gather.15.cloned.1.call-start = ((), (), s32[]{:S(2)}) async-start(), calls=%async_computation.11 | async-start | bytes 3538944 | tf_op jit(solution)/shard_map/all_gather | solution.py:279
  495.1 9.9 %collective-permute-start.14 = (bf16[192,768]{1,0:T(8,128)(2,1)S(1)}, bf16[192,768]{1,0:T(8,128)(2,1)S(1)}, u32[]{:S(2)}, u32[]{:S(2)}) collective-permute-start(bf16[192,768]{1,0:T(8,128)(2,1)S(1)} %pad_maximum_fusion.6), channel_id=1, source_target_pairs={{0,8},{4,12},{8,0},{12,4},{16,24},{20,28},{24,16},{28,20},{1,9},{5... | collective-permute-start | bytes 884744 | tf_op jit(solution)/shard_map/ppermute | solution.py:98
  497.7 12.4 %collective-permute-start.11 = (bf16[192,768]{1,0:T(8,128)(2,1)S(1)}, bf16[192,768]{1,0:T(8,128)(2,1)S(1)}, u32[]{:S(2)}, u32[]{:S(2)}) collective-permute-start(bf16[192,768]{1,0:T(8,128)(2,1)S(1)} %pad_maximum_fusion.5), channel_id=1, source_target_pairs={{0,8},{4,12},{8,0},{12,4},{16,24},{20,28},{24,16},{28,20},{1,9},{5... | collective-permute-start | bytes 884744 | tf_op jit(solution)/shard_map/ppermute | solution.py:98
  506.0 5.0 collective-permute-start.15
  511.0 2.2 collective-permute-start.12
  513.4 16.2 %copy-start.9 = (f32[512,768]{1,0:T(8,128)S(1)}, f32[512,768]{1,0:T(8,128)}, u32[]{:S(2)}) copy-start(f32[512,768]{1,0:T(8,128)} %copy-done.8) | copy-start | bytes 4718596
  513.5 16.2 %copy-start.14 = (bf16[12,64,512]{2,1,0:T(8,128)(2,1)S(1)}, bf16[12,64,512]{2,1,0:T(8,128)(2,1)}, u32[]{:S(2)}) copy-start(bf16[12,64,512]{2,1,0:T(8,128)(2,1)} %copy-done.13) | copy-start | bytes 2359300
  575.4 4.4 copy-start.1
  (17 other events, 19.3 us)
Sparse Core Ops, SparseCore 0:
  11.4 56.8 all-gather.12
  112.6 62.2 all-gather.8
  199.0 59.0 reduce-scatter.4
  266.1 63.3 all-gather.10
  346.4 59.0 reduce-scatter.6
  443.2 47.9 reduce-scatter.8
  494.1 35.4 reduce-scatter.10
  531.5 31.0 all-gather.14
where the time goes:
time: 597 us; the launch traced here: 587 us
  waiting for transfers between devices  353 us (59%)
  matrix products  89.3 us (15%)
  other arithmetic  58.8 us (10%)
  local copies, waits for them, and re-layouts  46.3 us (8%)
  starting transfers between devices  24.3 us (4%)
  between operations  15.5 us (3%)
    all_gather x1, waiting for transfers between devices, per_device(): ffn_rows = lax.all_gather(middle_low, 'tensor', axis=0, tiled=True)  61 us
    reduce_scatter x1, waiting for transfers between devices, per_device(): lax.psum_scatter(jnp.dot(hidden, down_weight, preferred_element_type=jnp....  59.1 us
    all_gather x1, waiting for transfers between devices, per_device(): mine = lax.all_gather(mine, 'tensor', axis=0, tiled=False)  56.9 us
    all_gather x1, waiting for transfers between devices, per_device(): branch_rows = lax.all_gather(branch_grad, 'tensor', axis=0, tiled=True)  52.3 us
    ppermute x9, waiting for transfers between devices, dp_halve(): got = lax.ppermute(give, 'dp', [(i, i ^ 1 << step) for i in range(dp_size)])  37.6 us
    all_gather x1, waiting for transfers between devices, per_device(): joined = lax.all_gather(joined, 'dp', axis=0, tiled=False)  27.7 us
    dot_general x5, matrix products, contract(): lax.dot_general(left, right, (((left_dim,), (right_dim,)), ((), ())), pre...  25.7 us
    reduce_scatter x1, waiting for transfers between devices, per_device(): lax.psum_scatter(grad_qkv_full.reshape(3 * width, width).astype(jnp.bfloa...  25.5 us
  transfers between devices with their start and end apart: 24, of which 19 were waited for; matrix products, arithmetic and copies ran while one was open for 8% of the time, Pallas kernels for 0%

commit v1 on v0

--- a/solution.py
+++ b/solution.py
@@ -7,6 +7,28 @@
 LEN = 512
 EPS = 1e-12
 NEG = -1e30
+
+
+def joined_along(blocks, dim):
+    lengths = list(blocks.shape[1:])
+    lengths[dim] *= blocks.shape[0]
+    return jnp.moveaxis(blocks, 0, dim).reshape(lengths)
+
+
+def doubled(x, axis):
+    length = lax.axis_size(axis)
+    blocks = x[None]
+    for level in range(length.bit_length() - 1):
+        bit = 1 << level
+        other = lax.ppermute(blocks, axis, [(i, i ^ bit) for i in range(length)])
+        both = jnp.stack([blocks, other])
+        upper = lax.axis_index(axis) >> level & 1
+        blocks = jnp.where(upper == 0, both, both[::-1]).reshape(-1, *x.shape)
+    return blocks
+
+
+def gather_by_bits(x, axis, dim):
+    return joined_along(doubled(x, axis), dim)
 
 
 def layer_norm(values, gain_vec, shift_vec):
@@ -165,7 +187,7 @@
             layer_norm, own_tokens + attn_out + out_bias, norm1_gain, norm1_shift
         )
         middle_low = middle.astype(jnp.bfloat16)
-        ffn_rows = lax.all_gather(middle_low, "tensor", axis=0, tiled=True)
+        ffn_rows = gather_by_bits(middle_low, "tensor", 0)
         pre_act = jnp.dot(ffn_rows, up_weight, preferred_element_type=jnp.float32) + up_bias
         activated, gelu_back = jax.vjp(gelu_exact, pre_act)
         hidden = activated.astype(jnp.bfloat16)

time: 597 us -> 633 us (1.060)
  waiting for transfers between devices: 353 us -> 380 us
  other arithmetic: 58.8 us -> 66.6 us
    ppermute x0 -> x2, waiting for transfers between devices: none -> 88.2 us  [doubled(): other = lax.ppermute(blocks, axis, [(i, i ^ bit) for i in range(length)])]
    all_gather x1 -> x0, waiting for transfers between devices: 61 us -> none  [per_device(): ffn_rows = lax.all_gather(middle_low, 'tensor', axis=0, tiled=True)]
    unnamed x122 -> x124, local copies, waits for them, and re-layouts: 16.4 us -> 15.9 us
  transfers between devices with their start and end apart: 24 -> 25, of which waited for: 19 -> 20; matrix products, arithmetic and copies ran while one was open for 8% -> 8% of each run, Pallas kernels for 0% -> 0%
where the time goes in v1:
time: 633 us; the launch traced here: 622 us
  waiting for transfers between devices  380 us (60%)
  matrix products  89.3 us (14%)
  other arithmetic  66.6 us (11%)
  local copies, waits for them, and re-layouts  45.7 us (7%)
  starting transfers between devices  25.4 us (4%)
  between operations  15.5 us (2%)
    ppermute x2, waiting for transfers between devices, doubled(): other = lax.ppermute(blocks, axis, [(i, i ^ bit) for i in range(length)])  88.2 us
    reduce_scatter x1, waiting for transfers between devices, per_device(): lax.psum_scatter(jnp.dot(hidden, down_weight, preferred_element_type=jnp....  59.2 us
    all_gather x1, waiting for transfers between devices, per_device(): mine = lax.all_gather(mine, 'tensor', axis=0, tiled=False)  56.9 us
    all_gather x1, waiting for transfers between devices, per_device(): branch_rows = lax.all_gather(branch_grad, 'tensor', axis=0, tiled=True)  52.3 us
    ppermute x9, waiting for transfers between devices, dp_halve(): got = lax.ppermute(give, 'dp', [(i, i ^ 1 << step) for i in range(dp_size)])  37.6 us
    all_gather x1, waiting for transfers between devices, per_device(): joined = lax.all_gather(joined, 'dp', axis=0, tiled=False)  27.7 us
    dot_general x5, matrix products, contract(): lax.dot_general(left, right, (((left_dim,), (right_dim,)), ((), ())), pre...  25.7 us
    reduce_scatter x1, waiting for transfers between devices, per_device(): lax.psum_scatter(grad_qkv_full.reshape(3 * width, width).astype(jnp.bfloa...  25.5 us
  transfers between devices with their start and end apart: 25, of which 20 were waited for; matrix products, arithmetic and copies ran while one was open for 8% of the time, Pallas kernels for 0%

profile of v1, /device:TPU:0, one launch (start us, length us, event | category | flops | bytes accessed | tf_op | source)
XLA Modules:
  0.0 622.3 jit_solution(9044541020246240394)
XLA Ops:
  9.4 1.8 fusion.43
  11.3 56.9 %all-gather.10.cloned.1.call-done = bf16[4,1544,192]{1,2,0:T(8,128)(2,1)} async-done(((bf16[1,1544,192]{1,2,0:T(8,128)(2,1)}), bf16[4,1544,192]{1,2,0:T(8,128)(2,1)}) %all-gather.10.cloned.1.call-update) | async-done | bytes 2371600 | tf_op jit(solution)/shard_map/all_gather | solution.py:159
  70.0 3.4 collective-permute-done
  73.4 3.0 broadcast_select_fusion.1
  78.2 2.0 fusion.19
  80.4 1.5 fusion.58
  83.8 5.0 fusion
  88.9 2.6 exponential_reduce_fusion
  91.5 1.9 copy-done.2
  93.5 10.1 %fusion.1 = bf16[12,512,512]{1,2,0:T(8,128)(2,1)} fusion(f32[12,512,512]{1,2,0:T(8,128)} %copy-done.2, f32[12,512]{1,0:T(8,128)S(1)} %log_add_fusion, pred[512]{0:T(512)(128)(4,1)S(1)} %copy-done.39), kind=kLoop, calls=%fused_computation.7 | loop fusion | flops 12582912 | bytes 18899456 | tf_op jit(solution)/shard_map/convert_element_type | solution.py:60
  103.6 4.1 convolution_convert_fusion.5
  107.8 2.7 fusion.60
  112.9 19.6 %collective-permute-done.1 = bf16[1,512,768]{2,1,0:T(8,128)(2,1)} collective-permute-done((bf16[1,512,768]{2,1,0:T(8,128)(2,1)}, bf16[1,512,768]{2,1,0:T(8,128)(2,1)}, u32[]{:S(2)}, u32[]{:S(2)}) %collective-permute-start.1) | collective-permute-done | bytes 786464 | tf_op jit(solution)/shard_map/ppermute | solution.py:23
  133.8 2.0 fusion.38
  137.7 68.6 %collective-permute-done.2 = bf16[2,512,768]{2,1,0:T(8,128)(2,1)} collective-permute-done((bf16[2,512,768]{2,1,0:T(8,128)(2,1)}, bf16[2,512,768]{2,1,0:T(8,128)(2,1)}, u32[]{:S(2)}, u32[]{:S(2)}) %collective-permute-start.2) | collective-permute-done | bytes 1572896 | tf_op jit(solution)/shard_map/ppermute | solution.py:23
  206.3 2.2 pad_maximum_fusion.1
  209.1 18.4 %multiply_convert_fusion.1 = (bf16[2048,768]{1,0:T(8,128)(2,1)S(1)}, f32[2048,768]{1,0:T(8,128)}, f32[2048,768]{1,0:T(8,128)}) fusion(f32[768]{0:T(1024)S(1)} %convert_element_type.191, bf16[2048,768]{1,0:T(8,128)(2,1)S(1)} %bitcast.169, bf16[768,768]{1,0:T(8,128)(2,1)S(1)} %copy-done), kind=kOutput, calls=%fused_computation.11 | convolution fusion | flops 2519728128 | bytes 20057088 | tf_op jit(solution)/shard_map/dot_general | solution.py:191
  227.5 1.7 copy-done.50
  229.2 3.9 convolution_convert_fusion.1
  233.2 59.2 %reduce-scatter.5.cloned.1.call-done = bf16[512,768]{1,0:T(8,128)(2,1)} async-done(((bf16[2048,768]{1,0:T(8,128)(2,1)}), bf16[512,768]{1,0:T(8,128)(2,1)}) %reduce-scatter.5.cloned.1.call-update) | async-done | bytes 786448 | tf_op jit(solution)/shard_map/reduce_scatter | solution.py:194
  292.4 1.8 fusion.56
  294.6 2.0 fusion.25
  296.6 1.6 fusion.55
  299.4 1.7 convert_reduce_fusion.3
  301.1 11.2 %reduce-scatter.7.cloned.1.call-start = ((), (), s32[]{:S(2)}) async-start(), calls=%async_computation.6 | async-start | bytes 3932160 | tf_op jit(solution)/shard_map/reduce_scatter | solution.py:218
  312.3 52.3 %all-gather.8.cloned.1.call-done = bf16[2048,768]{1,0:T(8,128)(2,1)} async-done(((bf16[512,768]{1,0:T(8,128)(2,1)}), bf16[2048,768]{1,0:T(8,128)(2,1)}) %all-gather.8.cloned.1.call-update) | async-done | bytes 3145744 | tf_op jit(solution)/shard_map/all_gather | solution.py:206
  364.6 11.0 %convert_reduce_fusion = (f32[768]{0:T(1024)}, bf16[2048,768]{1,0:T(8,128)(2,1)S(1)}) fusion(f32[2048,768]{1,0:T(8,128)} %get-tuple-element.89, f32[2048,768]{1,0:T(8,128)} %get-tuple-element.128, f32[768]{0:T(1024)} %copy-done.42, bf16[2048,768]{1,0:T(8,128)(2,1)} %all-gather.8.cloned.1.call-done, bf16[768,768]{1,0:T(8,128)(2,1)} %param.26), kind=kOutput, calls=%fused_computation.9 | convolution fusion | flops 2442657024 | bytes 20060160 | tf_op jit(solution)/shard_map/dot_general | solution.py:45
  375.6 1.7 copy-done.52
  377.3 4.0 convolution_convert_fusion
  381.5 5.7 fusion.61
  387.2 2.7 fusion.62
  392.3 2.5 collective-permute-done.6
  394.8 1.8 dynamic-slice_add_fusion
  402.8 11.1 %collective-permute-done.7 = f32[192,768]{1,0:T(8,128)} collective-permute-done((f32[192,768]{1,0:T(8,128)}, f32[192,768]{1,0:T(8,128)}, u32[]{:S(2)}, u32[]{:S(2)}) %collective-permute-start.7) | collective-permute-done | bytes 589856 | tf_op jit(solution)/shard_map/ppermute | solution.py:105
  417.3 8.4 %collective-permute-done.4 = f32[192,768]{1,0:T(8,128)} collective-permute-done((f32[192,768]{1,0:T(8,128)}, f32[192,768]{1,0:T(8,128)}, u32[]{:S(2)}, u32[]{:S(2)}) %collective-permute-start.4) | collective-permute-done | bytes 589856 | tf_op jit(solution)/shard_map/ppermute | solution.py:105
  429.1 2.9 slice.148
  432.0 1.7 dynamic-slice_add_fusion.4
  433.6 2.5 collective-permute-done.5
  436.1 1.7 dynamic-slice_add_fusion.5
  437.8 2.8 reduce-scatter.7.cloned.1.call-done
  440.6 2.0 convert_add_fusion
  446.0 2.9 convolution_convert_fusion.4
  450.6 10.3 %multiply_reduce_fusion = (f32[12,512]{1,0:T(8,128)S(1)}, f32[12,512,512]{1,2,0:T(8,128)}) fusion(f32[12,512,512]{1,2,0:T(8,128)S(1)} %bitcast.147, f32[12,512]{1,0:T(8,128)S(1)} %copy-done.26, pred[512]{0:T(512)(128)(4,1)S(1)} %copy-done.40, bf16[512,12,64]{0,2,1:T(8,128)(2,1)S(1)} %bitcast.159, f32[512,12,64]{0,2,1:T(8,128)S(1)} %bitcast.151, ...), kind=kOutput, calls=%fused_computation.1 | convolution fusion | flops 419162112 | bytes 27577856 | tf_op jit(solution)/shard_map/pqhe,pkhe->phqk/dot_general | solution.py:68
  460.9 7.2 %multiply_convert_fusion = bf16[12,512,512]{1,2,0:T(8,128)(2,1)S(1)} fusion(f32[12,512,512]{1,2,0:T(8,128)} %get-tuple-element.130, f32[12,512,512]{1,2,0:T(8,128)S(1)} %bitcast.147, f32[12,512]{1,0:T(8,128)S(1)} %get-tuple-element.129, f32[12,512]{1,0:T(8,128)S(1)} %copy-done.26, pred[512]{0:T(512)(128)(4,1)S(1)} %copy-done.40), kind=kLoop, calls=%fused_computation | loop fusion | flops 18874368 | bytes 31506944 | tf_op jit(solution)/shard_map/convert_element_type | solution.py:72
  468.2 2.1 multiply_convert_fusion.2
  473.4 4.9 convolution_convert_fusion.2
  481.7 2.2 fusion.28
  484.3 2.0 collective-permute-done.9
  488.1 7.5 %collective-permute-done.10 = bf16[192,768]{1,0:T(8,128)(2,1)S(1)} collective-permute-done((bf16[192,768]{1,0:T(8,128)(2,1)S(1)}, bf16[192,768]{1,0:T(8,128)(2,1)S(1)}, u32[]{:S(2)}, u32[]{:S(2)}) %collective-permute-start.10) | collective-permute-done | bytes 294944 | tf_op jit(solution)/shard_map/ppermute | solution.py:105
  497.2 3.7 collective-permute-done.11
  500.9 25.5 %reduce-scatter.9.cloned.1.call-done = bf16[288,768]{1,0:T(8,128)(2,1)} async-done(((bf16[2304,768]{1,0:T(8,128)(2,1)}), bf16[288,768]{1,0:T(8,128)(2,1)}) %reduce-scatter.9.cloned.1.call-update) | async-done | bytes 442384 | tf_op jit(solution)/shard_map/reduce_scatter | solution.py:280
  527.6 1.6 copy.94
  530.4 1.5 collective-permute-start.16
  533.6 6.7 %collective-permute-done.16 = bf16[192,768]{1,0:T(8,128)(2,1)S(1)} collective-permute-done((bf16[192,768]{1,0:T(8,128)(2,1)S(1)}, bf16[192,768]{1,0:T(8,128)(2,1)S(1)}, u32[]{:S(2)}, u32[]{:S(2)}) %collective-permute-start.16) | collective-permute-done | bytes 294944 | tf_op jit(solution)/shard_map/ppermute | solution.py:120
  541.3 4.1 collective-permute-done.13
  546.5 1.6 maximum_convert_fusion.1
  548.7 1.6 maximum_convert_fusion
  550.3 14.5 %reduce-scatter.11.cloned.1.call-done = f32[1,416,192]{1,2,0:T(8,128)} async-done(((f32[4,416,192]{1,2,0:T(8,128)}), f32[1,416,192]{1,2,0:T(8,128)}) %reduce-scatter.11.cloned.1.call-update) | async-done | bytes 319504 | tf_op jit(solution)/shard_map/reduce_scatter | solution.py:287
  564.9 5.2 fusion.26
  570.1 27.7 %all-gather.12.cloned.1.call-done = f32[8,416,192]{1,2,0:T(8,128)} async-done(((f32[1,416,192]{1,2,0:T(8,128)}), f32[8,416,192]{1,2,0:T(8,128)}) %all-gather.12.cloned.1.call-update) | async-done | bytes 2555920 | tf_op jit(solution)/shard_map/all_gather | solution.py:301
  605.2 3.2 slice.149
  608.4 2.2 copy.95
  610.6 1.8 copy.103
  612.5 1.5 slice_bitcast_fusion.1
  (253 shorter events, 61.3 us)
Async XLA Ops:
  7.2 201.9 %copy-start = (bf16[768,768]{1,0:T(8,128)(2,1)S(1)}, bf16[768,768]{1,0:T(8,128)(2,1)}, u32[]{:S(2)}) copy-start(bf16[768,768]{1,0:T(8,128)(2,1)} %param.24) | copy-start | bytes 3538948
  7.2 61.1 %copy-start.49 = (s32[4]{0:T(128)S(1)}, s32[4]{0:T(128)}, u32[]{:S(2)}) copy-start(s32[4]{0:T(128)} %param.17) | copy-start | bytes 52
  7.2 61.1 %all-gather.10.cloned.1.call-start = ((), (), s32[]{:S(2)}) async-start(), calls=%async_computation.9 | async-start | bytes 3194880 | tf_op jit(solution)/shard_map/all_gather | solution.py:159
  11.3 281.1 %reduce-scatter.5.cloned.1.call-start = ((), (), s32[]{:S(2)}) async-start(), calls=%async_computation.4 | async-start | bytes 3932160 | tf_op jit(solution)/shard_map/reduce_scatter | solution.py:194
  68.3 5.2 collective-permute-start
  77.9 2.4 copy-start.12
  81.9 21.7 %copy-start.4 = (f32[1,512,4,192]{1,3,0,2:T(8,128)}, f32[1,512,4,192]{1,3,0,2:T(8,128)S(1)}, u32[]{:S(2)}) copy-start(f32[1,512,4,192]{1,3,0,2:T(8,128)S(1)} %get-tuple-element.92) | copy-start | bytes 4718596
  83.1 20.5 %copy-start.30 = (f32[12,64]{1,0:T(8,128)}, f32[12,64]{1,0:T(8,128)S(1)}, u32[]{:S(2)}) copy-start(f32[12,64]{1,0:T(8,128)S(1)} %reshape.339) | copy-start | bytes 9220
  83.8 5.0 copy-start.28
  83.8 5.1 copy-start.39
  88.9 4.6 copy-start.2
  93.5 10.1 %copy-start.25 = (f32[12,512]{1,0:T(8,128)}, f32[12,512]{1,0:T(8,128)S(1)}, u32[]{:S(2)}) copy-start(f32[12,512]{1,0:T(8,128)S(1)} %log_add_fusion) | copy-start | bytes 73732
  103.6 4.1 copy-start.47
  103.6 4.1 copy-start.48
  107.7 2.8 copy-start.17
  107.7 3.7 copy-start.27
  107.7 3.7 copy-start.32
  112.6 19.9 %collective-permute-start.1 = (bf16[1,512,768]{2,1,0:T(8,128)(2,1)}, bf16[1,512,768]{2,1,0:T(8,128)(2,1)}, u32[]{:S(2)}, u32[]{:S(2)}) collective-permute-start(bf16[1,512,768]{2,1,0:T(8,128)(2,1)} %fusion.90), channel_id=1, source_target_pairs={{0,1},{1,0},{2,3},{3,2},{4,5},{5,4},{6,7},{7,6},{8,9},{9,8},{10,11... | collective-permute-start | bytes 2359304 | tf_op jit(solution)/shard_map/ppermute | solution.py:23
  135.8 70.5 %collective-permute-start.2 = (bf16[2,512,768]{2,1,0:T(8,128)(2,1)}, bf16[2,512,768]{2,1,0:T(8,128)(2,1)}, u32[]{:S(2)}, u32[]{:S(2)}) collective-permute-start(bf16[2,512,768]{2,1,0:T(8,128)(2,1)} %get-tuple-element.104), channel_id=1, source_target_pairs={{0,2},{1,3},{2,0},{3,1},{4,6},{5,7},{6,4},{7,5},{8,10},{9,11},{10,... | collective-permute-start | bytes 4718600 | tf_op jit(solution)/shard_map/ppermute | solution.py:23
  137.7 71.4 %copy-start.42 = (f32[768]{0:T(1024)}, f32[768]{0:T(1024)S(1)}, u32[]{:S(2)}) copy-start(f32[768]{0:T(1024)S(1)} %convert_element_type.191) | copy-start | bytes 9220
  209.0 18.5 %copy-start.15 = (bf16[2,2,512,768]{3,2,1,0:T(8,128)(2,1)}, bf16[2,2,512,768]{3,2,1,0:T(8,128)(2,1)S(1)}, u32[]{:S(2)}) copy-start(bf16[2,2,512,768]{3,2,1,0:T(8,128)(2,1)S(1)} %reverse_select_fusion) | copy-start | bytes 9437188
  209.1 20.1 %copy-start.45 = (bf16[768,768]{1,0:T(8,128)(2,1)S(1)}, bf16[768,768]{1,0:T(8,128)(2,1)}, u32[]{:S(2)}) copy-start(bf16[768,768]{1,0:T(8,128)(2,1)} %param.26) | copy-start | bytes 3538948
  233.2 131.4 %all-gather.8.cloned.1.call-start = ((), (), s32[]{:S(2)}) async-start(), calls=%async_computation.5 | async-start | bytes 3932160 | tf_op jit(solution)/shard_map/all_gather | solution.py:206
  301.1 139.5 %reduce-scatter.7.cloned.1.call-start = ((), (), s32[]{:S(2)}) async-start(), calls=%async_computation.6 | async-start | bytes 3932160 | tf_op jit(solution)/shard_map/reduce_scatter | solution.py:218
  381.4 145.1 %reduce-scatter.9.cloned.1.call-start = ((), (), s32[]{:S(2)}) async-start(), calls=%async_computation.7 | async-start | bytes 3981312 | tf_op jit(solution)/shard_map/reduce_scatter | solution.py:280
  381.4 5.7 copy-start.44
  381.5 5.7 copy-start.51
  387.2 2.8 copy-start.19
  391.8 3.0 collective-permute-start.6
  391.8 7.1 %collective-permute-start.3 = (f32[384,768]{1,0:T(8,128)}, f32[384,768]{1,0:T(8,128)}, u32[]{:S(2)}, u32[]{:S(2)}) collective-permute-start(f32[384,768]{1,0:T(8,128)} %get-tuple-element.132), channel_id=1, source_target_pairs={{0,4},{4,0},{8,12},{12,8},{16,20},{20,16},{24,28},{28,24},{1,5},{5... | collective-permute-start | bytes 3538952 | tf_op jit(solution)/shard_map/ppermute | solution.py:105
  392.3 6.6 %copy-start.20 = (f32[768,768]{1,0:T(8,128)S(1)}, f32[768,768]{1,0:T(8,128)}, u32[]{:S(2)}) copy-start(f32[768,768]{1,0:T(8,128)} %copy-done.19) | copy-start | bytes 7077892
  397.4 16.5 %collective-permute-start.7 = (f32[192,768]{1,0:T(8,128)}, f32[192,768]{1,0:T(8,128)}, u32[]{:S(2)}, u32[]{:S(2)}) collective-permute-start(f32[192,768]{1,0:T(8,128)} %constant_dynamic-slice_fusion.1), channel_id=1, source_target_pairs={{0,8},{4,12},{8,0},{12,4},{16,24},{20,28},{24,16},{28,20},{1,9},{5... | collective-permute-start | bytes 1769480 | tf_op jit(solution)/shard_map/ppermute | solution.py:105
  402.2 23.5 %collective-permute-start.4 = (f32[192,768]{1,0:T(8,128)}, f32[192,768]{1,0:T(8,128)}, u32[]{:S(2)}, u32[]{:S(2)}) collective-permute-start(f32[192,768]{1,0:T(8,128)} %constant_dynamic-slice_fusion.4), channel_id=1, source_target_pairs={{0,8},{4,12},{8,0},{12,4},{16,24},{20,28},{24,16},{28,20},{1,9},{5... | collective-permute-start | bytes 1769480 | tf_op jit(solution)/shard_map/ppermute | solution.py:105
  402.8 23.0 %copy-start.11 = (f32[384,768]{1,0:T(8,128)S(1)}, f32[384,768]{1,0:T(8,128)}, u32[]{:S(2)}) copy-start(f32[384,768]{1,0:T(8,128)} %copy-done.10) | copy-start | bytes 3538948
  415.0 11.8 %copy-start.22 = (f32[192,768]{1,0:T(8,128)}, f32[192,768]{1,0:T(8,128)S(1)}, u32[]{:S(2)}) copy-start(f32[192,768]{1,0:T(8,128)S(1)} %dynamic-slice_add_fusion.2) | copy-start | bytes 1769476
  415.9 16.1 %collective-permute-start.8 = (f32[96,768]{1,0:T(8,128)}, f32[96,768]{1,0:T(8,128)}, u32[]{:S(2)}, u32[]{:S(2)}) collective-permute-start(f32[96,768]{1,0:T(8,128)} %constant_dynamic-slice_fusion), channel_id=1, source_target_pairs={{0,16},{4,20},{8,24},{12,28},{16,0},{20,4},{24,8},{28,12},{1,17},{... | collective-permute-start | bytes 884744 | tf_op jit(solution)/shard_map/ppermute | solution.py:105
  427.6 4.4 copy-start.23
  427.6 8.5 %collective-permute-start.5 = (f32[96,768]{1,0:T(8,128)}, f32[96,768]{1,0:T(8,128)}, u32[]{:S(2)}, u32[]{:S(2)}) collective-permute-start(f32[96,768]{1,0:T(8,128)} %constant_dynamic-slice_fusion.3), channel_id=1, source_target_pairs={{0,16},{4,20},{8,24},{12,28},{16,0},{20,4},{24,8},{28,12},{1,17},{... | collective-permute-start | bytes 884744 | tf_op jit(solution)/shard_map/ppermute | solution.py:105
  440.6 4.9 slice-start.3
  443.3 2.6 slice-start.4
  443.3 5.6 slice-start
  444.6 4.3 slice-start.1
  445.9 4.2 slice-start.2
  445.9 4.6 copy-start.5
  445.9 4.6 copy-start.26
  445.9 4.6 copy-start.31
  445.9 4.6 copy-start.40
  460.9 7.3 %copy-start.7 = (f32[1,512,4,192]{1,3,0,2:T(8,128)S(1)}, f32[1,512,4,192]{1,3,0,2:T(8,128)}, u32[]{:S(2)}) copy-start(f32[1,512,4,192]{1,3,0,2:T(8,128)} %get-tuple-element.93) | copy-start | bytes 4718596
  460.9 7.3 %copy-start.29 = (f32[12,64]{1,0:T(8,128)S(1)}, f32[12,64]{1,0:T(8,128)}, u32[]{:S(2)}) copy-start(f32[12,64]{1,0:T(8,128)} %copy-done.28) | copy-start | bytes 9220
  470.2 2.6 copy-start.13
  478.3 86.5 %reduce-scatter.11.cloned.1.call-start = ((), (), s32[]{:S(2)}) async-start(), calls=%async_computation.8 | async-start | bytes 1966080 | tf_op jit(solution)/shard_map/reduce_scatter | solution.py:287
  479.6 52.3 %collective-permute-start.12 = (bf16[96,768]{1,0:T(8,128)(2,1)}, bf16[96,768]{1,0:T(8,128)(2,1)}, u32[]{:S(2)}, u32[]{:S(2)}) collective-permute-start(bf16[96,768]{1,0:T(8,128)(2,1)} %dynamic-slice_add_fusion.5), channel_id=1, source_target_pairs={{0,16},{4,20},{8,24},{12,28},{16,0},{20,4},{24,8},{28,12},{1,17},{... | collective-permute-start | bytes 442376 | tf_op jit(solution)/shard_map/ppermute | solution.py:120
  481.0 48.3 %collective-permute-start.15 = (bf16[96,768]{1,0:T(8,128)(2,1)}, bf16[96,768]{1,0:T(8,128)(2,1)}, u32[]{:S(2)}, u32[]{:S(2)}) collective-permute-start(bf16[96,768]{1,0:T(8,128)(2,1)} %dynamic-slice_add_fusion.4), channel_id=1, source_target_pairs={{0,16},{4,20},{8,24},{12,28},{16,0},{20,4},{24,8},{28,12},{1,17},{... | collective-permute-start | bytes 442376 | tf_op jit(solution)/shard_map/ppermute | solution.py:120
  483.9 2.4 collective-permute-start.9
  486.5 9.1 %collective-permute-start.10 = (bf16[192,768]{1,0:T(8,128)(2,1)S(1)}, bf16[192,768]{1,0:T(8,128)(2,1)S(1)}, u32[]{:S(2)}, u32[]{:S(2)}) collective-permute-start(bf16[192,768]{1,0:T(8,128)(2,1)S(1)} %dynamic-slice_convert_fusion.1), channel_id=1, source_target_pairs={{0,8},{4,12},{8,0},{12,4},{16,24},{20,28},{24,16},{28,20},{1,9},{5... | collective-permute-start | bytes 884744 | tf_op jit(solution)/shard_map/ppermute | solution.py:105
  495.7 5.2 collective-permute-start.11
  529.3 68.5 %all-gather.12.cloned.1.call-start = ((), (), s32[]{:S(2)}) async-start(), calls=%async_computation.10 | async-start | bytes 3538944 | tf_op jit(solution)/shard_map/all_gather | solution.py:301
  530.4 9.9 %collective-permute-start.16 = (bf16[192,768]{1,0:T(8,128)(2,1)S(1)}, bf16[192,768]{1,0:T(8,128)(2,1)S(1)}, u32[]{:S(2)}, u32[]{:S(2)}) collective-permute-start(bf16[192,768]{1,0:T(8,128)(2,1)S(1)} %pad_maximum_fusion.8), channel_id=1, source_target_pairs={{0,8},{4,12},{8,0},{12,4},{16,24},{20,28},{24,16},{28,20},{1,9},{5... | collective-permute-start | bytes 884744 | tf_op jit(solution)/shard_map/ppermute | solution.py:120
  532.9 12.4 %collective-permute-start.13 = (bf16[192,768]{1,0:T(8,128)(2,1)S(1)}, bf16[192,768]{1,0:T(8,128)(2,1)S(1)}, u32[]{:S(2)}, u32[]{:S(2)}) collective-permute-start(bf16[192,768]{1,0:T(8,128)(2,1)S(1)} %pad_maximum_fusion.7), channel_id=1, source_target_pairs={{0,8},{4,12},{8,0},{12,4},{16,24},{20,28},{24,16},{28,20},{1,9},{5... | collective-permute-start | bytes 884744 | tf_op jit(solution)/shard_map/ppermute | solution.py:120
  541.3 5.0 collective-permute-start.17
  546.3 2.2 collective-permute-start.14
  548.7 16.2 %copy-start.9 = (f32[512,768]{1,0:T(8,128)S(1)}, f32[512,768]{1,0:T(8,128)}, u32[]{:S(2)}) copy-start(f32[512,768]{1,0:T(8,128)} %copy-done.8) | copy-start | bytes 4718596
  548.7 16.2 %copy-start.14 = (bf16[12,64,512]{2,1,0:T(8,128)(2,1)S(1)}, bf16[12,64,512]{2,1,0:T(8,128)(2,1)}, u32[]{:S(2)}) copy-start(bf16[12,64,512]{2,1,0:T(8,128)(2,1)} %copy-done.13) | copy-start | bytes 2359300
  610.6 4.4 copy-start.1
  (19 other events, 25.9 us)
Sparse Core Ops, SparseCore 0:
  11.4 56.8 all-gather.9
  233.3 59.0 reduce-scatter.4
  301.2 63.3 all-gather.7
  381.5 59.0 reduce-scatter.6
  478.5 47.9 reduce-scatter.8
  529.4 35.4 reduce-scatter.10
  566.7 31.0 all-gather.11
